TPU v7x, 256 devices: a whole 4x4x8 slice. The times are simulated.
256 devices in a mesh: row: 32 (over y, x, core), col: 8 (over z).
Axes of the slice: x: 4, y: 4, z: 8, core: 2. Of those that a mesh axis runs over, the one named last changes fastest.
Arguments:
- covariance: float32 [8192, 8192], P('row', 'col'), may hold values from 0 to 4, as said below
- panels: int32 [4], replicated, may hold values from 0 to 31, as said below
- observed: float32 [8192], P('row'), may hold values from -6 to 6
- drift_basis: float32 [64, 8192], P(None, 'row'), may hold values from -1.5 to 1.5
Outputs:
- complement: float32 [8192, 8192], P('row', 'col')
- factor: float32 [8192, 1024], P('row')
- solved_data: float32 [8192], P('row')
- solved_drift: float32 [64, 8192], P(None, 'row')
Inputs may be any that keep to these rules, and one draw needn't show every extreme that they name: `covariance`: symmetric and positive definite. `panels`: 4 different tile indices; tile 32 - 1 is always among them.
All inputs are finite; a program needn't handle non-finite values.
Results may differ from a plain program's by a relative error of at most 0.0003.
Values sent between devices are 32-bit elements; how exact they have to be, the bound alone decides.
No kernel may reach another device: no remote copies, remote signals or barrier semaphores. Data moves between devices by JAX's collectives and lax.ppermute only.
A program may use at most 64 MiB of HBM per device.

v0:
```python
import jax
import jax.numpy as jnp
from jax import lax
from jax.sharding import PartitionSpec as P

B = 256
K = 4
HIGH = lax.Precision.HIGHEST


def keep_mask(tiles, chosen):
    return jnp.all(tiles[:, None] != chosen[None, :], axis=1).astype(jnp.float32)


def dot(a, b):
    return lax.dot_general(a, b, (((1,), (0,)), ((), ())), precision=HIGH)


def dot_nt(a, b):
    return lax.dot_general(a, b, (((1,), (1,)), ((), ())), precision=HIGH)


def panel_keep(tiles, panels):
    cols = []
    for p in range(K):
        cols.append(jnp.broadcast_to(keep_mask(tiles, panels[:p])[:, None], (tiles.shape[0], B)))
    return jnp.concatenate(cols, axis=1)


def on_device(covariance, panels, observed, drift_basis):
    rows_here = covariance.shape[0]
    cols_here = covariance.shape[1]
    r = lax.axis_index("row")
    row_start = r * rows_here
    col_start = lax.axis_index("col") * cols_here
    row_tiles = (row_start + lax.iota(jnp.int32, rows_here)) // B
    col_tiles = (col_start + lax.iota(jnp.int32, cols_here)) // B
    sides = jnp.concatenate([observed[None, :], drift_basis], axis=0)
    with jax.named_scope("gather_row_strip"):
        strip = lax.all_gather(covariance, "col", axis=1, tiled=True)
        panel_cols = jnp.concatenate(
            [lax.dynamic_slice_in_dim(strip, panels[j] * B, B, 1) for j in range(K)], axis=1
        )
    with jax.named_scope("share_panel_rows"):
        s_rows, a_rows, w_cols = ([], [], [])
        for j in range(K):
            off = panels[j] * B - row_start
            mine = (off >= 0) & (off < rows_here)
            off = jnp.clip(off, 0, rows_here - B)
            s_rows.append(jnp.where(mine, lax.dynamic_slice_in_dim(panel_cols, off, B, 0), 0.0))
            a_rows.append(jnp.where(mine, lax.dynamic_slice_in_dim(covariance, off, B, 0), 0.0))
            w_cols.append(jnp.where(mine, lax.dynamic_slice_in_dim(sides, off, B, 1), 0.0))
        rows_buf = jnp.concatenate(
            [jnp.concatenate(s_rows, axis=0), jnp.concatenate(a_rows, axis=0)], axis=1
        )
        w_buf = jnp.concatenate(w_cols, axis=1)
        rows_buf, w_buf = lax.psum((rows_buf, w_buf), "row")
        s_full = rows_buf[:, : K * B]
        a_panel_rows = rows_buf[:, K * B :]
    with jax.named_scope("block_cholesky"):
        chol = jnp.linalg.cholesky(s_full)
    with jax.named_scope("forward_solves"):
        rhs = jnp.concatenate([panel_cols, w_buf], axis=0)
        solved = lax.linalg.triangular_solve(
            chol, rhs, left_side=False, lower=True, transpose_a=True
        )
        factor_rows = solved[:rows_here] * panel_keep(row_tiles, panels)
        z = solved[rows_here:]
        factor_cols_t = (
            lax.linalg.triangular_solve(
                chol, a_panel_rows, left_side=True, lower=True, transpose_a=False
            )
            * panel_keep(col_tiles, panels).T
        )
    with jax.named_scope("complement_update"):
        final_rows = keep_mask(row_tiles, panels)
        final_cols = keep_mask(col_tiles, panels)
        complement = (
            (covariance - dot(factor_rows, factor_cols_t))
            * final_rows[:, None]
            * final_cols[None, :]
        )
    with jax.named_scope("sides_update"):
        new_sides = sides - dot_nt(z, factor_rows)
        for j in range(K):
            off = panels[j] * B - row_start
            placed = lax.dynamic_update_slice_in_dim(
                jnp.zeros_like(new_sides),
                z[:, j * B : (j + 1) * B],
                jnp.clip(off, 0, rows_here - B),
                1,
            )
            new_sides = jnp.where((row_tiles == panels[j])[None, :], placed, new_sides)
    return (complement, factor_rows, new_sides[0], new_sides[1:])


def solution(mesh):
    return jax.shard_map(
        on_device,
        mesh=mesh,
        in_specs=(P("row", "col"), P(), P("row"), P(None, "row")),
        out_specs=(P("row", "col"), P("row", None), P("row"), P(None, "row")),
        check_vma=False,
    )
```

profile of v0, /device:TPU:1, one launch (start us, length us, event | category | flops | bytes accessed | tf_op | source)
XLA Modules:
  0.0 680.8 jit_solution(17626151562019785900)
XLA Ops:
  7.2 2.5 copy.43
  18.5 89.9 %all-gather.2.cloned.1.call-done = f32[256,8192]{0,1:T(8,128)} async-done(((f32[256,1024]{0,1:T(8,128)}), f32[256,8192]{0,1:T(8,128)}) %all-gather.2.cloned.1.call-update) | async-done | bytes 8388624 | tf_op jit(solution)/shard_map/gather_row_strip/all_gather | solution.py:40
  110.6 10.2 %maximum_maximum_fusion = f32[1024,2048]{0,1:T(8,128)} fusion(f32[256,1024]{0,1:T(8,128)S(1)} %get-tuple-element.46, f32[256,1024]{0,1:T(8,128)S(1)} %copy-done.4, f32[256,1024]{0,1:T(8,128)S(1)} %copy-done.5, f32[256,1024]{0,1:T(8,128)S(1)} %get-tuple-element.45, f32[256,1024]{0,1:T(8,128)S(1)} %broadcast_select_fusion.4, ...), kind=kLoop, calls=%fused_computation.2 | loop fusion | flops 14680064 | bytes 16777216 | tf_op jit(solution)/shard_map/share_panel_rows/concatenate | solution.py:53
  130.0 122.0 %all-reduce.4.cloned.1.call-done = (f32[65,1024]{0,1:T(8,128)}, f32[1024,2048]{0,1:T(8,128)}) async-done(((f32[65,1024]{0,1:T(8,128)}, f32[1024,2048]{0,1:T(8,128)}), (f32[65,1024]{0,1:T(8,128)}, f32[1024,2048]{0,1:T(8,128)})) %all-reduce.4.cloned.1.call-update) | async-done | bytes 8654864 | tf_op jit(solution)/shard_map/share_panel_rows/psum | solution.py:57
  252.0 4.7 slice.373
  256.7 5.8 copy.50
  262.6 4.4 fusion.8
  269.0 11.7 %cholesky.223 = f32[128,128]{1,0:T(8,128)S(1)} custom-call(f32[128,128]{1,0:T(8,128)S(1)} %cholesky.580), custom_call_target="Cholesky" | custom-call | tf_op jit(solution)/shard_map/block_cholesky/jit(cholesky)/cholesky | solution.py:61
  280.7 2.5 cholesky.255
  283.2 9.8 %custom-call.64 = f32[1,128,128]{1,2,0:T(8,128)S(1)} custom-call(f32[1,128,128]{2,1,0:T(8,128)S(1)} %get-tuple-element.123), custom_call_target="InvertDiagBlocksLowerTriangular" | custom-call | tf_op jit(solution)/shard_map/block_cholesky/jit(cholesky)/cholesky | solution.py:61
  293.0 2.4 constant_dynamic-update-slice_fusion.51
  297.0 11.9 %cholesky.244 = f32[128,128]{1,0:T(8,128)S(1)} custom-call(f32[128,128]{1,0:T(8,128)S(1)} %cholesky.584), custom_call_target="Cholesky" | custom-call | tf_op jit(solution)/shard_map/block_cholesky/jit(cholesky)/cholesky | solution.py:61
  309.5 9.8 %custom-call.65 = f32[1,128,128]{1,2,0:T(8,128)S(1)} custom-call(f32[1,128,128]{2,1,0:T(8,128)S(1)} %get-tuple-element.120), custom_call_target="InvertDiagBlocksLowerTriangular" | custom-call | tf_op jit(solution)/shard_map/block_cholesky/jit(cholesky)/cholesky | solution.py:61
  322.7 11.7 %cholesky.468 = f32[128,128]{1,0:T(8,128)S(1)} custom-call(f32[128,128]{1,0:T(8,128)S(1)} %cholesky.589), custom_call_target="Cholesky" | custom-call | tf_op jit(solution)/shard_map/block_cholesky/jit(cholesky)/cholesky | solution.py:61
  335.7 9.8 %custom-call.66 = f32[1,128,128]{1,2,0:T(8,128)S(1)} custom-call(f32[1,128,128]{2,1,0:T(8,128)S(1)} %get-tuple-element.117), custom_call_target="InvertDiagBlocksLowerTriangular" | custom-call | tf_op jit(solution)/shard_map/block_cholesky/jit(cholesky)/cholesky | solution.py:61
  346.7 2.3 convolution_subtract_fusion.7
  349.0 11.9 %cholesky.487 = f32[128,128]{1,0:T(8,128)S(1)} custom-call(f32[128,128]{1,0:T(8,128)S(1)} %cholesky.594), custom_call_target="Cholesky" | custom-call | tf_op jit(solution)/shard_map/block_cholesky/jit(cholesky)/cholesky | solution.py:61
  362.3 9.8 %custom-call.67 = f32[1,128,128]{1,2,0:T(8,128)S(1)} custom-call(f32[1,128,128]{2,1,0:T(8,128)S(1)} %get-tuple-element.114), custom_call_target="InvertDiagBlocksLowerTriangular" | custom-call | tf_op jit(solution)/shard_map/block_cholesky/jit(cholesky)/cholesky | solution.py:61
  373.2 2.3 convolution_subtract_fusion.8
  375.5 11.7 %cholesky.506 = f32[128,128]{1,0:T(8,128)S(1)} custom-call(f32[128,128]{1,0:T(8,128)S(1)} %cholesky.599), custom_call_target="Cholesky" | custom-call | tf_op jit(solution)/shard_map/block_cholesky/jit(cholesky)/cholesky | solution.py:61
  388.6 10.2 %custom-call.68 = f32[1,128,128]{1,2,0:T(8,128)S(1)} custom-call(f32[1,128,128]{2,1,0:T(8,128)S(1)} %get-tuple-element.111), custom_call_target="InvertDiagBlocksLowerTriangular" | custom-call | tf_op jit(solution)/shard_map/block_cholesky/jit(cholesky)/cholesky | solution.py:61
  399.8 2.3 convolution_subtract_fusion.16
  402.1 11.7 %cholesky.526 = f32[128,128]{1,0:T(8,128)S(1)} custom-call(f32[128,128]{1,0:T(8,128)S(1)} %cholesky.604), custom_call_target="Cholesky" | custom-call | tf_op jit(solution)/shard_map/block_cholesky/jit(cholesky)/cholesky | solution.py:61
  415.2 9.8 %custom-call.69 = f32[1,128,128]{1,2,0:T(8,128)S(1)} custom-call(f32[1,128,128]{2,1,0:T(8,128)S(1)} %get-tuple-element.108), custom_call_target="InvertDiagBlocksLowerTriangular" | custom-call | tf_op jit(solution)/shard_map/block_cholesky/jit(cholesky)/cholesky | solution.py:61
  428.0 11.9 %cholesky.546 = f32[128,128]{1,0:T(8,128)S(1)} custom-call(f32[128,128]{1,0:T(8,128)S(1)} %cholesky.609), custom_call_target="Cholesky" | custom-call | tf_op jit(solution)/shard_map/block_cholesky/jit(cholesky)/cholesky | solution.py:61
  441.2 9.8 %custom-call.70 = f32[1,128,128]{1,2,0:T(8,128)S(1)} custom-call(f32[1,128,128]{2,1,0:T(8,128)S(1)} %get-tuple-element.105), custom_call_target="InvertDiagBlocksLowerTriangular" | custom-call | tf_op jit(solution)/shard_map/block_cholesky/jit(cholesky)/cholesky | solution.py:61
  453.6 11.7 %cholesky.564 = f32[128,128]{1,0:T(8,128)S(1)} custom-call(f32[128,128]{1,0:T(8,128)S(1)} %convolution_subtract_fusion.19), custom_call_target="Cholesky" | custom-call | tf_op jit(solution)/shard_map/block_cholesky/jit(cholesky)/cholesky | solution.py:61
  472.3 4.9 select_select_fusion
  477.2 22.5 %while.1 = (s32[]{:T(128)}, f32[1024,1024]{1,0:T(8,128)}, s32[8,2]{0,1:T(2,128)S(1)}, f32[8,128,128]{2,1,0:T(8,128)S(1)}, s32[]{:T(128)}) while((s32[]{:T(128)}, f32[1024,1024]{1,0:T(8,128)}, s32[8,2]{0,1:T(2,128)S(1)}, f32[8,128,128]{2,1,0:T(8,128)S(1)}, s32[]{:T(128)}) %tuple.106), condition=%wide.while_cond, body=%wide.while_body.sunk | while | flops 2 | bytes 131181 | solution.py:64
  477.8 2.2 bitcast_dynamic-update-slice_fusion.2
  480.6 2.2 bitcast_dynamic-update-slice_fusion.2
  494.8 2.2 bitcast_dynamic-update-slice_fusion.2
  499.8 78.8 %custom-call.71 = f32[8,128,128]{1,2,0:T(8,128)S(1)} custom-call(f32[8,128,128]{2,1,0:T(8,128)S(1)} %get-tuple-element.11), custom_call_target="InvertDiagBlocksLowerTriangular" | custom-call | tf_op jit(solution)/shard_map/forward_solves/triangular_solve | solution.py:64
  590.2 2.5 convolution_subtract_fusion.11
  595.3 2.3 constant_dynamic-update-slice_fusion.13
  597.6 2.3 convolution_subtract_fusion.15
  601.2 2.5 convolution_subtract_fusion.10
  605.0 2.7 convolution_subtract_fusion.9
  612.5 2.4 fusion.42
  615.7 3.2 constant_dynamic-update-slice_fusion.43
  619.6 2.5 convolution_subtract_fusion.4
  624.2 2.9 convolution_subtract_fusion
  629.3 3.8 fusion.33
  635.3 4.6 fusion.36
  642.1 6.4 convolution_subtract_fusion.2
  650.4 7.3 %convolution_subtract_fusion.1 = f32[128,1024]{0,1:T(8,128)S(1)} fusion(f32[768,1024]{1,0:T(8,128)} %get-tuple-element.53, f32[1024,2048]{0,1:T(8,128)} %get-tuple-element.33, f32[1024,1024]{1,0:T(8,128)} %get-tuple-element.202), kind=kOutput, calls=%fused_computation.37 | convolution fusion | flops 1208090624 | bytes 4587520 | tf_op jit(solution)/shard_map/forward_solves/triangular_solve | solution.py:70
  659.2 8.5 %convolution_subtract_fusion.3 = f32[128,1024]{0,1:T(8,128)S(1)} fusion(f32[896,1024]{1,0:T(8,128)} %get-tuple-element.49, f32[1024,2048]{0,1:T(8,128)} %get-tuple-element.33, f32[1024,1024]{1,0:T(8,128)} %get-tuple-element.202), kind=kOutput, calls=%fused_computation.41 | convolution fusion | flops 1409417216 | bytes 5177344 | tf_op jit(solution)/shard_map/forward_solves/triangular_solve | solution.py:70
  668.7 5.0 fusion.30
  (174 shorter events, 94.2 us)
Async XLA Ops:
  7.2 101.2 %all-gather.2.cloned.1.call-start = ((), (), s32[]{:S(2)}) async-start(), calls=%async_computation | async-start | bytes 9437184 | tf_op jit(solution)/shard_map/gather_row_strip/all_gather | solution.py:40
  9.7 7.0 %copy-start.1 = (f32[256,1024]{0,1:T(8,128)S(1)}, f32[256,1024]{0,1:T(8,128)}, u32[]{:S(2)}) copy-start(f32[256,1024]{0,1:T(8,128)} %copy.43) | copy-start | bytes 3145732
  9.8 242.2 %all-reduce.4.cloned.1.call-start = ((), (), s32[]{:S(2)}) async-start(), calls=%async_computation.1 | async-start | bytes 17825792 | tf_op jit(solution)/shard_map/share_panel_rows/psum | solution.py:57
  18.5 92.1 %copy-start.4 = (f32[256,1024]{0,1:T(8,128)S(1)}, f32[256,1024]{0,1:T(8,128)}, u32[]{:S(2)}) copy-start(f32[256,1024]{0,1:T(8,128)} %get-tuple-element.47) | copy-start | bytes 3145732
  108.3 2.2 copy-start.5
  109.7 0.7 copy-start.6
  109.7 0.8 copy-start.8
  109.7 0.9 copy-start.10
  120.8 0.7 copy-start.14
  267.0 2.0 copy-start
  472.3 106.3 %copy-start.7 = (f32[256,256]{0,1:T(8,128)S(1)}, f32[256,256]{0,1:T(8,128)}, u32[]{:S(2)}) copy-start(f32[256,256]{0,1:T(8,128)} %copy-done.6) | copy-start | bytes 786436
  472.3 106.3 %copy-start.9 = (f32[256,256]{0,1:T(8,128)S(1)}, f32[256,256]{0,1:T(8,128)}, u32[]{:S(2)}) copy-start(f32[256,256]{0,1:T(8,128)} %copy-done.8) | copy-start | bytes 786436
  472.3 106.3 %copy-start.11 = (f32[256,256]{0,1:T(8,128)S(1)}, f32[256,256]{0,1:T(8,128)}, u32[]{:S(2)}) copy-start(f32[256,256]{0,1:T(8,128)} %copy-done.10) | copy-start | bytes 786436
  589.6 0.7 copy-start.13
  597.6 13.2 %copy-start.16 = (f32[256]{0:T(256)S(1)}, f32[256]{0:T(256)}, u32[]{:S(2)}) copy-start(f32[256]{0:T(256)} %get-tuple-element.143) | copy-start | bytes 3076
  599.8 11.1 %copy-start.21 = (f32[256]{0:T(256)S(1)}, f32[256]{0:T(256)}, u32[]{:S(2)}) copy-start(f32[256]{0:T(256)} %convert_element_type.57) | copy-start | bytes 3076
  599.8 11.2 %copy-start.22 = (f32[256]{0:T(256)S(1)}, f32[256]{0:T(256)}, u32[]{:S(2)}) copy-start(f32[256]{0:T(256)} %convert_element_type.58) | copy-start | bytes 3076
  603.7 8.9 %copy-start.17 = (pred[256]{0:T(512)(128)(4,1)S(1)}, pred[256]{0:T(512)(128)(4,1)}, u32[]{:S(2)}) copy-start(pred[256]{0:T(512)(128)(4,1)} %get-tuple-element.145) | copy-start | bytes 772
  603.7 8.9 %copy-start.18 = (pred[256]{0:T(512)(128)(4,1)S(1)}, pred[256]{0:T(512)(128)(4,1)}, u32[]{:S(2)}) copy-start(pred[256]{0:T(512)(128)(4,1)} %get-tuple-element.146) | copy-start | bytes 772
  603.7 8.9 %copy-start.19 = (pred[256]{0:T(512)(128)(4,1)S(1)}, pred[256]{0:T(512)(128)(4,1)}, u32[]{:S(2)}) copy-start(pred[256]{0:T(512)(128)(4,1)} %get-tuple-element.144) | copy-start | bytes 772
  603.7 8.9 %copy-start.23 = (pred[256]{0:T(512)(128)(4,1)S(1)}, pred[256]{0:T(512)(128)(4,1)}, u32[]{:S(2)}) copy-start(pred[256]{0:T(512)(128)(4,1)} %broadcast_compare_fusion.3) | copy-start | bytes 772
  612.5 56.2 %copy-start.2 = (f32[256,1024]{1,0:T(8,128)}, f32[256,1024]{1,0:T(8,128)S(1)}, u32[]{:S(2)}) copy-start(f32[256,1024]{1,0:T(8,128)S(1)} %slice_multiply_fusion) | copy-start | bytes 3145732
  650.4 7.3 %copy-start.3 = (f32[1024,1024]{1,0:T(8,128)S(1)}, f32[1024,1024]{1,0:T(8,128)}, u32[]{:S(2)}) copy-start(f32[1024,1024]{1,0:T(8,128)} %get-tuple-element.52) | copy-start | bytes 12582916
  657.7 10.6 %copy-start.15 = (f32[1024]{0:T(1024)S(1)}, f32[1024]{0:T(1024)}, u32[]{:S(2)}) copy-start(f32[1024]{0:T(1024)} %compare_convert_fusion) | copy-start | bytes 12292
  659.2 9.5 %copy-start.12 = (f32[256,1024]{1,0:T(8,128)S(1)}, f32[256,1024]{1,0:T(8,128)}, u32[]{:S(2)}) copy-start(f32[256,1024]{1,0:T(8,128)} %param.4) | copy-start | bytes 3145732
  659.2 9.6 %copy-start.20 = (f32[256]{0:T(256)S(1)}, f32[256]{0:T(256)}, u32[]{:S(2)}) copy-start(f32[256]{0:T(256)} %convert_element_type.62) | copy-start | bytes 3076
Sparse Core Ops, SparseCore 0:
  10.4 97.9 all-gather.1
  121.0 130.9 all-reduce.3
where the time goes:
time: 688 us; the launch traced here: 681 us
  other arithmetic  285 us (41%)
  waiting for transfers between devices  212 us (31%)
  matrix products  108 us (16%)
  local copies, waits for them, and re-layouts  53.2 us (8%)
  between operations  22.7 us (3%)
    another operation x30, other arithmetic, on_device(): chol = jnp.linalg.cholesky(s_full)  172 us
    psum x1, waiting for transfers between devices, on_device(): rows_buf, w_buf = lax.psum((rows_buf, w_buf), 'row')  122 us
    all_gather x1, waiting for transfers between devices, on_device(): strip = lax.all_gather(covariance, 'col', axis=1, tiled=True)  89.9 us
    another operation x3, other arithmetic, on_device(): lax.linalg.triangular_solve(chol, rhs, left_side=False, lower=True, trans...  83.7 us
    another operation x15, matrix products, on_device(): lax.linalg.triangular_solve(chol, a_panel_rows, left_side=True, lower=Tru...  51.8 us
    another operation x15, matrix products, on_device(): lax.linalg.triangular_solve(chol, rhs, left_side=False, lower=True, trans...  25.6 us
    another operation x14, matrix products, on_device(): chol = jnp.linalg.cholesky(s_full)  23.1 us
    another operation x24, local copies, waits for them, and re-layouts  22.4 us
  transfers between devices with their start and end apart: 2, of which 2 were waited for; matrix products, arithmetic and copies ran while one was open for 2% of the time, Pallas kernels for 0%

commit v1 on v0

--- a/solution.py
+++ b/solution.py
@@ -37,7 +37,8 @@
     col_tiles = (col_start + lax.iota(jnp.int32, cols_here)) // B
     sides = jnp.concatenate([observed[None, :], drift_basis], axis=0)
     with jax.named_scope("gather_row_strip"):
-        strip = lax.all_gather(covariance, "col", axis=1, tiled=True)
+        outgoing = jnp.stack([covariance] * lax.axis_size("col"))
+        strip = jnp.concatenate(lax.all_to_all(outgoing, "col", 0, 0), axis=1)
         panel_cols = jnp.concatenate(
             [lax.dynamic_slice_in_dim(strip, panels[j] * B, B, 1) for j in range(K)], axis=1
         )

time: 688 us -> 787 us (1.14)
  waiting for transfers between devices: 212 us -> 301 us
  starting transfers between devices: 0.08 us -> 9.18 us
    all_to_all x0 -> x1, waiting for transfers between devices: none -> 181 us  [on_device(): strip = jnp.concatenate(lax.all_to_all(outgoing, 'col', 0, 0), axis=1)]
    all_gather x1 -> x0, waiting for transfers between devices: 89.9 us -> none  [on_device(): strip = lax.all_gather(covariance, 'col', axis=1, tiled=True)]
    all_to_all x0 -> x1, starting transfers between devices: none -> 9.15 us  [on_device(): strip = jnp.concatenate(lax.all_to_all(outgoing, 'col', 0, 0), axis=1)]
    another operation x24 -> x25, local copies, waits for them, and re-layouts: 22.4 us -> 27 us
where the time goes in v1:
time: 787 us; the launch traced here: 780 us
  waiting for transfers between devices  301 us (38%)
  other arithmetic  285 us (36%)
  matrix products  108 us (14%)
  local copies, waits for them, and re-layouts  54 us (7%)
  between operations  22.7 us (3%)
  starting transfers between devices  9.18 us (1%)
    all_to_all x1, waiting for transfers between devices, on_device(): strip = jnp.concatenate(lax.all_to_all(outgoing, 'col', 0, 0), axis=1)  181 us
    another operation x30, other arithmetic, on_device(): chol = jnp.linalg.cholesky(s_full)  172 us
    psum x1, waiting for transfers between devices, on_device(): rows_buf, w_buf = lax.psum((rows_buf, w_buf), 'row')  120 us
    another operation x3, other arithmetic, on_device(): lax.linalg.triangular_solve(chol, rhs, left_side=False, lower=True, trans...  83.7 us
    another operation x15, matrix products, on_device(): lax.linalg.triangular_solve(chol, a_panel_rows, left_side=True, lower=Tru...  51.8 us
    another operation x15, matrix products, on_device(): lax.linalg.triangular_solve(chol, rhs, left_side=False, lower=True, trans...  25.6 us
    another operation x14, matrix products, on_device(): chol = jnp.linalg.cholesky(s_full)  23.1 us
    another operation x24, local copies, waits for them, and re-layouts  23 us
  transfers between devices with their start and end apart: 2, of which 2 were waited for; matrix products, arithmetic and copies ran while one was open for 2% of the time, Pallas kernels for 0%

profile of v1, /device:TPU:1, one launch (start us, length us, event | category | flops | bytes accessed | tf_op | source)
XLA Modules:
  0.0 779.6 jit_solution(10412070366422848344)
XLA Ops:
  8.7 3.9 stack.2
  12.7 9.1 %all-to-all-start = ((f32[8,256,1024]{1,2,0:T(8,128)}), f32[8,256,1024]{1,2,0:T(8,128)}, u32[]{:S(2)}, u32[]{:S(2)}) async-start(f32[8,256,1024]{1,2,0:T(8,128)} %stack.2), calls=%async_computation | async-start | bytes 16777216 | tf_op jit(solution)/shard_map/gather_row_strip/all_to_all | solution.py:41
  28.0 180.9 %all-to-all-done = f32[8,256,1024]{1,2,0:T(8,128)} async-done(((f32[8,256,1024]{1,2,0:T(8,128)}), f32[8,256,1024]{1,2,0:T(8,128)}, u32[]{:S(2)}, u32[]{:S(2)}) %all-to-all-start) | async-done | bytes 8388640 | tf_op jit(solution)/shard_map/gather_row_strip/all_to_all | solution.py:41
  211.2 10.2 %maximum_maximum_fusion = f32[1024,2048]{0,1:T(8,128)} fusion(f32[256,1024]{0,1:T(8,128)S(1)} %get-tuple-element.46, f32[256,1024]{0,1:T(8,128)S(1)} %copy-done.3, f32[256,1024]{0,1:T(8,128)S(1)} %copy-done.4, f32[256,1024]{0,1:T(8,128)S(1)} %get-tuple-element.45, f32[256,1024]{0,1:T(8,128)S(1)} %broadcast_select_fusion.4, ...), kind=kLoop, calls=%fused_computation.2 | loop fusion | flops 14680064 | bytes 16777216 | tf_op jit(solution)/shard_map/share_panel_rows/concatenate | solution.py:54
  229.9 120.2 %all-reduce.4.cloned.1.call-done = (f32[65,1024]{0,1:T(8,128)}, f32[1024,2048]{0,1:T(8,128)}) async-done(((f32[65,1024]{0,1:T(8,128)}, f32[1024,2048]{0,1:T(8,128)}), (f32[65,1024]{0,1:T(8,128)}, f32[1024,2048]{0,1:T(8,128)})) %all-reduce.4.cloned.1.call-update) | async-done | bytes 8654864 | tf_op jit(solution)/shard_map/share_panel_rows/psum | solution.py:58
  350.1 4.7 slice.373
  354.9 5.8 copy.50
  360.7 4.4 fusion.8
  367.1 11.7 %cholesky.223 = f32[128,128]{1,0:T(8,128)S(1)} custom-call(f32[128,128]{1,0:T(8,128)S(1)} %cholesky.580), custom_call_target="Cholesky" | custom-call | tf_op jit(solution)/shard_map/block_cholesky/jit(cholesky)/cholesky | solution.py:62
  378.9 2.5 cholesky.255
  381.3 9.8 %custom-call.64 = f32[1,128,128]{1,2,0:T(8,128)S(1)} custom-call(f32[1,128,128]{2,1,0:T(8,128)S(1)} %get-tuple-element.123), custom_call_target="InvertDiagBlocksLowerTriangular" | custom-call | tf_op jit(solution)/shard_map/block_cholesky/jit(cholesky)/cholesky | solution.py:62
  391.2 2.4 constant_dynamic-update-slice_fusion.51
  395.1 11.9 %cholesky.244 = f32[128,128]{1,0:T(8,128)S(1)} custom-call(f32[128,128]{1,0:T(8,128)S(1)} %cholesky.584), custom_call_target="Cholesky" | custom-call | tf_op jit(solution)/shard_map/block_cholesky/jit(cholesky)/cholesky | solution.py:62
  407.6 9.8 %custom-call.65 = f32[1,128,128]{1,2,0:T(8,128)S(1)} custom-call(f32[1,128,128]{2,1,0:T(8,128)S(1)} %get-tuple-element.120), custom_call_target="InvertDiagBlocksLowerTriangular" | custom-call | tf_op jit(solution)/shard_map/block_cholesky/jit(cholesky)/cholesky | solution.py:62
  420.8 11.7 %cholesky.468 = f32[128,128]{1,0:T(8,128)S(1)} custom-call(f32[128,128]{1,0:T(8,128)S(1)} %cholesky.589), custom_call_target="Cholesky" | custom-call | tf_op jit(solution)/shard_map/block_cholesky/jit(cholesky)/cholesky | solution.py:62
  433.8 9.8 %custom-call.66 = f32[1,128,128]{1,2,0:T(8,128)S(1)} custom-call(f32[1,128,128]{2,1,0:T(8,128)S(1)} %get-tuple-element.117), custom_call_target="InvertDiagBlocksLowerTriangular" | custom-call | tf_op jit(solution)/shard_map/block_cholesky/jit(cholesky)/cholesky | solution.py:62
  444.8 2.3 convolution_subtract_fusion.7
  447.1 11.9 %cholesky.487 = f32[128,128]{1,0:T(8,128)S(1)} custom-call(f32[128,128]{1,0:T(8,128)S(1)} %cholesky.594), custom_call_target="Cholesky" | custom-call | tf_op jit(solution)/shard_map/block_cholesky/jit(cholesky)/cholesky | solution.py:62
  460.4 9.8 %custom-call.67 = f32[1,128,128]{1,2,0:T(8,128)S(1)} custom-call(f32[1,128,128]{2,1,0:T(8,128)S(1)} %get-tuple-element.114), custom_call_target="InvertDiagBlocksLowerTriangular" | custom-call | tf_op jit(solution)/shard_map/block_cholesky/jit(cholesky)/cholesky | solution.py:62
  471.3 2.3 convolution_subtract_fusion.8
  473.7 11.7 %cholesky.506 = f32[128,128]{1,0:T(8,128)S(1)} custom-call(f32[128,128]{1,0:T(8,128)S(1)} %cholesky.599), custom_call_target="Cholesky" | custom-call | tf_op jit(solution)/shard_map/block_cholesky/jit(cholesky)/cholesky | solution.py:62
  486.8 10.2 %custom-call.68 = f32[1,128,128]{1,2,0:T(8,128)S(1)} custom-call(f32[1,128,128]{2,1,0:T(8,128)S(1)} %get-tuple-element.111), custom_call_target="InvertDiagBlocksLowerTriangular" | custom-call | tf_op jit(solution)/shard_map/block_cholesky/jit(cholesky)/cholesky | solution.py:62
  500.3 11.7 %cholesky.526 = f32[128,128]{1,0:T(8,128)S(1)} custom-call(f32[128,128]{1,0:T(8,128)S(1)} %cholesky.604), custom_call_target="Cholesky" | custom-call | tf_op jit(solution)/shard_map/block_cholesky/jit(cholesky)/cholesky | solution.py:62
  513.3 9.8 %custom-call.69 = f32[1,128,128]{1,2,0:T(8,128)S(1)} custom-call(f32[1,128,128]{2,1,0:T(8,128)S(1)} %get-tuple-element.108), custom_call_target="InvertDiagBlocksLowerTriangular" | custom-call | tf_op jit(solution)/shard_map/block_cholesky/jit(cholesky)/cholesky | solution.py:62
  526.1 11.9 %cholesky.546 = f32[128,128]{1,0:T(8,128)S(1)} custom-call(f32[128,128]{1,0:T(8,128)S(1)} %cholesky.609), custom_call_target="Cholesky" | custom-call | tf_op jit(solution)/shard_map/block_cholesky/jit(cholesky)/cholesky | solution.py:62
  539.3 9.8 %custom-call.70 = f32[1,128,128]{1,2,0:T(8,128)S(1)} custom-call(f32[1,128,128]{2,1,0:T(8,128)S(1)} %get-tuple-element.105), custom_call_target="InvertDiagBlocksLowerTriangular" | custom-call | tf_op jit(solution)/shard_map/block_cholesky/jit(cholesky)/cholesky | solution.py:62
  551.8 11.7 %cholesky.564 = f32[128,128]{1,0:T(8,128)S(1)} custom-call(f32[128,128]{1,0:T(8,128)S(1)} %convolution_subtract_fusion.19), custom_call_target="Cholesky" | custom-call | tf_op jit(solution)/shard_map/block_cholesky/jit(cholesky)/cholesky | solution.py:62
  570.5 4.9 select_select_fusion
  575.4 23.2 %while.1 = (s32[]{:T(128)}, f32[1024,1024]{1,0:T(8,128)}, s32[8,2]{0,1:T(2,128)S(1)}, f32[8,128,128]{2,1,0:T(8,128)S(1)}, s32[]{:T(128)}) while((s32[]{:T(128)}, f32[1024,1024]{1,0:T(8,128)}, s32[8,2]{0,1:T(2,128)S(1)}, f32[8,128,128]{2,1,0:T(8,128)S(1)}, s32[]{:T(128)}) %tuple.106), condition=%wide.while_cond, body=%wide.while_body.sunk | while | flops 2 | bytes 131181 | solution.py:65
  576.0 2.3 bitcast_dynamic-update-slice_fusion.2
  578.9 2.3 bitcast_dynamic-update-slice_fusion.2
  584.7 2.3 bitcast_dynamic-update-slice_fusion.2
  587.6 2.3 bitcast_dynamic-update-slice_fusion.2
  590.6 2.3 bitcast_dynamic-update-slice_fusion.2
  598.6 78.8 %custom-call.71 = f32[8,128,128]{1,2,0:T(8,128)S(1)} custom-call(f32[8,128,128]{2,1,0:T(8,128)S(1)} %get-tuple-element.11), custom_call_target="InvertDiagBlocksLowerTriangular" | custom-call | tf_op jit(solution)/shard_map/forward_solves/triangular_solve | solution.py:65
  689.1 2.5 convolution_subtract_fusion.11
  700.0 2.5 convolution_subtract_fusion.10
  703.8 2.7 convolution_subtract_fusion.9
  711.4 2.4 fusion.42
  714.5 3.2 constant_dynamic-update-slice_fusion.43
  718.5 2.5 convolution_subtract_fusion.4
  723.1 2.9 convolution_subtract_fusion
  728.2 3.8 fusion.33
  734.2 4.6 fusion.36
  740.9 6.4 convolution_subtract_fusion.2
  749.2 7.3 convolution_subtract_fusion.1
  758.0 8.5 %convolution_subtract_fusion.3 = f32[128,1024]{0,1:T(8,128)S(1)} fusion(f32[896,1024]{1,0:T(8,128)} %get-tuple-element.49, f32[1024,2048]{0,1:T(8,128)} %get-tuple-element.33, f32[1024,1024]{1,0:T(8,128)} %get-tuple-element.203), kind=kOutput, calls=%fused_computation.41 | convolution fusion | flops 1409417216 | bytes 5177344 | tf_op jit(solution)/shard_map/forward_solves/triangular_solve | solution.py:71
  767.6 5.0 fusion.30
  (176 shorter events, 95.3 us)
Async XLA Ops:
  12.7 9.2 %copy-start.14 = (s32[4]{0:T(128)S(1)}, s32[4]{0:T(128)}, u32[]{:S(2)}) copy-start(s32[4]{0:T(128)} %param.5) | copy-start | bytes 52
  12.7 12.4 %copy-start.20 = (f32[256]{0:T(256)S(1)}, f32[256]{0:T(256)}, u32[]{:S(2)}) copy-start(f32[256]{0:T(256)} %param.6) | copy-start | bytes 3076
  12.7 12.5 %copy-start.13 = (f32[64,256]{1,0:T(8,128)S(1)}, f32[64,256]{1,0:T(8,128)}, u32[]{:S(2)}) copy-start(f32[64,256]{1,0:T(8,128)} %param.7) | copy-start | bytes 196612
  12.7 196.2 %all-to-all-start = ((f32[8,256,1024]{1,2,0:T(8,128)}), f32[8,256,1024]{1,2,0:T(8,128)}, u32[]{:S(2)}, u32[]{:S(2)}) async-start(f32[8,256,1024]{1,2,0:T(8,128)} %stack.2), calls=%async_computation | async-start | bytes 16777216 | tf_op jit(solution)/shard_map/gather_row_strip/all_to_all | solution.py:41
  21.8 328.3 %all-reduce.4.cloned.1.call-start = ((), (), s32[]{:S(2)}) async-start(), calls=%async_computation.1 | async-start | bytes 17825792 | tf_op jit(solution)/shard_map/share_panel_rows/psum | solution.py:58
  208.9 2.3 copy-start.3
  208.9 2.3 copy-start.4
  210.3 0.7 copy-start.5
  210.3 0.8 copy-start.7
  210.3 0.9 copy-start.9
  365.1 2.0 copy-start
  570.5 107.0 %copy-start.6 = (f32[256,256]{0,1:T(8,128)S(1)}, f32[256,256]{0,1:T(8,128)}, u32[]{:S(2)}) copy-start(f32[256,256]{0,1:T(8,128)} %copy-done.5) | copy-start | bytes 786436
  570.5 107.0 %copy-start.8 = (f32[256,256]{0,1:T(8,128)S(1)}, f32[256,256]{0,1:T(8,128)}, u32[]{:S(2)}) copy-start(f32[256,256]{0,1:T(8,128)} %copy-done.7) | copy-start | bytes 786436
  570.5 107.0 %copy-start.10 = (f32[256,256]{0,1:T(8,128)S(1)}, f32[256,256]{0,1:T(8,128)}, u32[]{:S(2)}) copy-start(f32[256,256]{0,1:T(8,128)} %copy-done.9) | copy-start | bytes 786436
  688.4 0.7 copy-start.12
  696.4 13.2 %copy-start.16 = (f32[256]{0:T(256)S(1)}, f32[256]{0:T(256)}, u32[]{:S(2)}) copy-start(f32[256]{0:T(256)} %get-tuple-element.143) | copy-start | bytes 3076
  698.7 11.1 %copy-start.22 = (f32[256]{0:T(256)S(1)}, f32[256]{0:T(256)}, u32[]{:S(2)}) copy-start(f32[256]{0:T(256)} %convert_element_type.57) | copy-start | bytes 3076
  698.7 11.2 %copy-start.23 = (f32[256]{0:T(256)S(1)}, f32[256]{0:T(256)}, u32[]{:S(2)}) copy-start(f32[256]{0:T(256)} %convert_element_type.58) | copy-start | bytes 3076
  702.5 8.9 %copy-start.17 = (pred[256]{0:T(512)(128)(4,1)S(1)}, pred[256]{0:T(512)(128)(4,1)}, u32[]{:S(2)}) copy-start(pred[256]{0:T(512)(128)(4,1)} %get-tuple-element.145) | copy-start | bytes 772
  702.5 8.9 %copy-start.18 = (pred[256]{0:T(512)(128)(4,1)S(1)}, pred[256]{0:T(512)(128)(4,1)}, u32[]{:S(2)}) copy-start(pred[256]{0:T(512)(128)(4,1)} %get-tuple-element.146) | copy-start | bytes 772
  702.5 8.9 %copy-start.19 = (pred[256]{0:T(512)(128)(4,1)S(1)}, pred[256]{0:T(512)(128)(4,1)}, u32[]{:S(2)}) copy-start(pred[256]{0:T(512)(128)(4,1)} %get-tuple-element.144) | copy-start | bytes 772
  702.5 8.9 %copy-start.24 = (pred[256]{0:T(512)(128)(4,1)S(1)}, pred[256]{0:T(512)(128)(4,1)}, u32[]{:S(2)}) copy-start(pred[256]{0:T(512)(128)(4,1)} %broadcast_compare_fusion.3) | copy-start | bytes 772
  711.4 56.2 %copy-start.1 = (f32[256,1024]{1,0:T(8,128)}, f32[256,1024]{1,0:T(8,128)S(1)}, u32[]{:S(2)}) copy-start(f32[256,1024]{1,0:T(8,128)S(1)} %slice_multiply_fusion) | copy-start | bytes 3145732
  749.2 7.3 copy-start.2
  756.5 10.6 %copy-start.15 = (f32[1024]{0:T(1024)S(1)}, f32[1024]{0:T(1024)}, u32[]{:S(2)}) copy-start(f32[1024]{0:T(1024)} %compare_convert_fusion) | copy-start | bytes 12292
  758.0 9.5 %copy-start.11 = (f32[256,1024]{1,0:T(8,128)S(1)}, f32[256,1024]{1,0:T(8,128)}, u32[]{:S(2)}) copy-start(f32[256,1024]{1,0:T(8,128)} %param.4) | copy-start | bytes 3145732
  758.0 9.6 %copy-start.21 = (f32[256]{0:T(256)S(1)}, f32[256]{0:T(256)}, u32[]{:S(2)}) copy-start(f32[256]{0:T(256)} %convert_element_type.62) | copy-start | bytes 3076
Sparse Core Ops, SparseCore 0:
  221.6 128.4 all-reduce.3
